TPU v7x, 32 devices: a whole 2x2x4 slice. The times are simulated.
32 devices in a mesh: groups: 2 (over x), blk: 8 (over z, y), inner: 2 (over core).
Axes of the slice: x: 2, y: 2, z: 4, core: 2. Of those that a mesh axis runs over, the one named last changes fastest.
Arguments:
- patch_rows: bfloat16 [24576, 1536], P(('groups', 'blk', 'inner')), parts along dimension 0, may hold values from -6 to 6
- owner_ids: int32 [24576, 1], P(('groups', 'blk', 'inner')), parts along dimension 0, may hold values from 0 to 7; in each aligned block of 768 rows (0 to 767, 768 to 1535, ...) at most 192 rows name the same one
- page_ids: int32 [24576], P(('groups', 'blk', 'inner')), parts along dimension 0, may hold values from 0 to 7
- proj_weight: bfloat16 [1536, 128], replicated, may hold values from -0.15625 to 0.15625
- proj_bias: float32 [128], replicated, may hold values from -1.8 to 1.8
- query_tokens: bfloat16 [128, 32, 128], P(('groups', 'blk')), parts along dimension 0, may hold values from -0.5 to 0.5
- query_counts: int32 [128], P(('groups', 'blk')), parts along dimension 0, may hold values from 1 to 32, as said below
Outputs:
- page_scores: float32 [256, 64], P(('groups', 'blk', 'inner')), parts along dimension 0
There are 2 independent parts, one for each index of `groups`. A program takes and returns all parts, laid end to end along the dimension named above; an argument that names none is the same for every part. Nothing has to cross between parts.
Inputs may be any that keep to these rules, and one draw needn't show every extreme that they name: `owner_ids`: among the rows of one device, at most 192 name the same owner, a bound that some block reaches of them. `query_counts`: the first query of each part has all 32 tokens live.
All inputs are finite; a program needn't handle non-finite values.
Results may differ from a plain program's by a relative error of at most 0.00031.
Values may be sent and summed in bfloat16 or wider, within the bound.
No kernel may reach another device: no remote copies, remote signals or barrier semaphores. Data moves between devices by JAX's collectives and lax.ppermute only.
A program may use at most 64 MiB of HBM per device.

v0:
```python
import math
import jax
import jax.numpy as jnp
from jax import lax
from jax.sharding import PartitionSpec as P

PAGES_DEV = 8


def embed(rows, weight, bias):
    proj = jnp.dot(rows, weight, preferred_element_type=jnp.float32) + bias[None, :]
    scale = lax.rsqrt(jnp.sum(proj * proj, axis=1, keepdims=True) + 1e-06)
    return (proj * scale).astype(jnp.bfloat16)


def page_maxsim(tokens, counts, embedded, slot_pages, token_slots, page_total):
    sims = jnp.einsum("re,se->rs", tokens, embedded, preferred_element_type=jnp.float32)
    best = jnp.stack(
        [
            jnp.max(jnp.where(slot_pages[None, :] == page, sims, jnp.float32(-2.0)), axis=1)
            for page in range(page_total)
        ],
        axis=0,
    )
    best = best.reshape(page_total, counts.shape[0], token_slots)
    live = (jnp.arange(token_slots, dtype=jnp.int32)[None, :] < counts[:, None]).astype(jnp.float32)
    return jnp.sum(best * live[None, :, :], axis=2)


def make_scorer(embedded, slot_pages, page_total, token_slots, width):

    def score_block(carry, pieces, start):
        tokens, counts = pieces
        count_q = tokens.shape[0]
        group = math.gcd(count_q, max(1, 512 // token_slots))
        token_blocks = tokens.reshape(count_q // group, group * token_slots, width)
        count_blocks = counts.reshape(count_q // group, group)

        def one_block(args):
            block_tokens, block_counts = args
            return page_maxsim(
                block_tokens, block_counts, embedded, slot_pages, token_slots, page_total
            )

        scored = lax.map(one_block, (token_blocks, count_blocks))
        scored = jnp.transpose(scored, (1, 0, 2)).reshape(page_total, count_q)
        return scored

    return score_block


def shards(patch_rows, owner_ids, page_ids, proj_weight, proj_bias, query_tokens, query_counts):
    owners = lax.axis_size("blk")
    rows = patch_rows.shape[0]
    capacity = 2 * rows // owners
    slot_count = owners * capacity
    target = owner_ids[:, 0]
    onehot = (target[:, None] == jnp.arange(owners, dtype=jnp.int32)[None, :]).astype(jnp.int32)
    before = jnp.sum((jnp.cumsum(onehot, axis=0) - onehot) * onehot, axis=1)
    slot_index = target * capacity + before
    outgoing_pages = jnp.full((slot_count,), -1, jnp.int32).at[slot_index].set(page_ids)
    local = embed(patch_rows, proj_weight, proj_bias)
    packed = jnp.zeros((slot_count, local.shape[1]), jnp.bfloat16).at[slot_index].set(local)
    embedded, slot_pages = (
        lax.all_to_all(packed, "blk", split_axis=0, concat_axis=0, tiled=True),
        lax.all_to_all(outgoing_pages, "blk", split_axis=0, concat_axis=0, tiled=True),
    )
    per_block = query_tokens.shape[0]
    token_slots = query_tokens.shape[1]
    width = query_tokens.shape[2]
    total_queries = per_block * owners
    initial = jnp.zeros((PAGES_DEV, total_queries), jnp.float32)
    scorer = make_scorer(embedded, slot_pages, PAGES_DEV, token_slots, width)
    return scorer(
        initial,
        (
            lax.all_gather(query_tokens, "blk", axis=0, tiled=True),
            lax.all_gather(query_counts, "blk", axis=0, tiled=True),
        ),
        jnp.int32(0),
    )


def solution(mesh):
    in_specs = (
        P(("groups", "blk", "inner"), None),
        P(("groups", "blk", "inner"), None),
        P(("groups", "blk", "inner")),
        P(),
        P(),
        P(("groups", "blk"), None, None),
        P(("groups", "blk")),
    )
    out_specs = P(("groups", "blk", "inner"), None)
    return jax.shard_map(shards, mesh=mesh, in_specs=in_specs, out_specs=out_specs, check_vma=False)
```

profile of v0, /device:TPU:0, one launch (start us, length us, event | category | flops | bytes accessed | tf_op | source)
XLA Modules:
  0.0 88.6 jit_solution(12246551596819438382)
XLA Ops:
  0.0 0.8 reduce
  0.9 1.7 %reduce-window.6 = s32[8,6,128]{2,0,1:T(8,128)S(1)} reduce-window(s32[8,6,128]{2,0,1:T(8,128)S(1)} %fusion.10, s32[]{:T(128)} %copy.41), window={size=1x1x128 pad=0_0x0_0x127_0}, to_apply=%region_0.0 | reduce-window | flops 780288 | bytes 49156 | tf_op jit(solution)/shard_map/reduce-window
  2.7 0.1 copy.20
  2.8 0.2 reduce-window.9
  3.0 0.1 copy.21
  3.0 0.1 fusion.9
  3.1 0.7 fusion.13
  3.8 3.5 %scatter_custom_fusion = s32[1536]{0:T(1024)S(1)} fusion(s32[768]{0:T(1024)S(1)} %fusion.13, s32[768]{0:T(1024)} %param.11, s32[]{:T(128)} %constant.17.clone.1), kind=kCustom, calls=%fused_computation.49 | custom fusion | bytes 6656 | tf_op jit(solution)/shard_map/scatter | solution.py:61
  7.4 0.7 all_to_all.22
  8.1 7.3 %all-to-all-start = ((s32[8,192,1]{1,2,0:T(1,128)}), s32[8,192,1]{1,2,0:T(1,128)S(1)}, u32[]{:S(2)}, u32[]{:S(2)}) async-start(s32[8,192,1]{1,2,0:T(1,128)} %all_to_all.22), calls=%async_computation | async-start | bytes 16384 | tf_op jit(solution)/shard_map/all_to_all | solution.py:66
  15.4 1.9 %multiply_reduce_fusion.1 = (f32[768]{0:T(1024)S(1)}, f32[768,128]{0,1:T(8,128)S(1)}) fusion(f32[128]{0:T(128)} %param.13, bf16[768,1536]{1,0:T(8,128)(2,1)S(1)} %copy-done, bf16[1536,128]{1,0:T(8,128)(2,1)} %param.12), kind=kOutput, calls=%fused_computation.38 | convolution fusion | flops 302284032 | bytes 3149312 | tf_op jit(solution)/shard_map/dot_general | solution.py:11
  17.4 0.2 copy.23
  17.6 5.0 %scatter_custom_fusion.1 = bf16[1536,128]{1,0:T(8,128)(2,1)} fusion(s32[768]{0:T(1024)S(1)} %fusion.13, bf16[768,128]{1,0:T(8,128)(2,1)S(1)} %copy.23, bf16[]{:T(256)} %constant.13.clone.1), kind=kCustom, calls=%fused_computation.39 | custom fusion | bytes 393218 | tf_op jit(solution)/shard_map/scatter | solution.py:63
  22.6 6.0 %all-to-all-start.1 = ((bf16[8,192,128]{2,1,0:T(8,128)(2,1)}), bf16[8,192,128]{2,1,0:T(8,128)(2,1)S(1)}, u32[]{:S(2)}, u32[]{:S(2)}) async-start(bf16[8,192,128]{2,1,0:T(8,128)(2,1)} %bitcast.7), calls=%async_computation.1 | async-start | bytes 786432 | tf_op jit(solution)/shard_map/all_to_all | solution.py:65
  28.6 0.6 dynamic-slice
  29.9 0.2 dynamic-update-slice
  30.1 12.5 %all-reduce = s32[64]{0:T(128)S(1)} all-reduce(s32[64]{0:T(128)S(1)} %dynamic-update-slice), channel_id=1, replica_groups=mesh['groups'=2,'blk'=8,'inner'=2] {'blk'}, use_global_device_ids=true, to_apply=%add | all-reduce | flops 64 | bytes 512
  42.6 0.1 reshape.110
  42.7 31.5 %all_gather.6 = bf16[64,32,128]{2,1,0:T(8,128)(2,1)S(1)} all-gather(bf16[8,32,128]{2,1,0:T(8,128)(2,1)S(1)} %copy-done.1), channel_id=1, replica_groups=mesh['groups'=2,'blk'=8,'inner'=2] {'blk'}, dimensions={0}, use_global_device_ids=true | all-gather | bytes 589824 | tf_op jit(solution)/shard_map/all_gather | solution.py:77
  74.3 13.6 %while.10 = (s32[]{:T(128)}, f32[4,8,16]{2,1,0:T(8,128)S(1)}, s32[1536]{0:T(1024)S(1)}, bf16[4,512,128]{2,1,0:T(8,128)(2,1)S(1)}, bf16[1536,128]{1,0:T(8,128)(2,1)S(1)}, /*index=5*/s32[4,16]{1,0:T(4,128)S(1)}, s32[]{:T(128)}) while((s32[]{:T(128)}, f32[4,8,16]{2,1,0:T(8,128)S(1)}, s32[1536]{0:T(1024)S(1)}, ...), condition=%wide.region_16.17_spmd, body=%wide.region_6.16_spmd.sunk | while | flops 213926784 | bytes 762649 | solution.py:45
  74.3 2.5 %select_reduce_fusion.9 = (f32[512]{0:T(512)S(1)}, f32[512]{0:T(512)S(1)}, f32[512]{0:T(512)S(1)}, f32[512]{0:T(512)S(1)}, f32[512]{0:T(512)S(1)}, /*index=5*/f32[512]{0:T(512)S(1)}, f32[512]{0:T(512)S(1)}, f32[512]{0:T(512)S(1)}) fusion(pred[1536]{0:T(1024)(128)(4,1)S(1)} %get-tuple-element.121, pred[1536]{0:T(1024)(128)(4,1)S(1)} %get-tuple-element.122, ...), kind=kOutput, calls=%fused_computation.2.clone.1 | convolution fusion | flops 213905408 | bytes 557060 | tf_op jit(solution)/shard_map/while/body/eval_jaxpr/re,se->rs/dot_general | solution.py:17
  76.8 0.1 stack.35
  77.5 0.1 multiply_reduce_fusion.3
  77.7 2.5 %select_reduce_fusion.9 = (f32[512]{0:T(512)S(1)}, f32[512]{0:T(512)S(1)}, f32[512]{0:T(512)S(1)}, f32[512]{0:T(512)S(1)}, f32[512]{0:T(512)S(1)}, /*index=5*/f32[512]{0:T(512)S(1)}, f32[512]{0:T(512)S(1)}, f32[512]{0:T(512)S(1)}) fusion(pred[1536]{0:T(1024)(128)(4,1)S(1)} %get-tuple-element.121, pred[1536]{0:T(1024)(128)(4,1)S(1)} %get-tuple-element.122, ...), kind=kOutput, calls=%fused_computation.2.clone.1 | convolution fusion | flops 213905408 | bytes 557060 | tf_op jit(solution)/shard_map/while/body/eval_jaxpr/re,se->rs/dot_general | solution.py:17
  80.2 0.1 stack.35
  80.9 0.1 multiply_reduce_fusion.3
  81.1 2.5 %select_reduce_fusion.9 = (f32[512]{0:T(512)S(1)}, f32[512]{0:T(512)S(1)}, f32[512]{0:T(512)S(1)}, f32[512]{0:T(512)S(1)}, f32[512]{0:T(512)S(1)}, /*index=5*/f32[512]{0:T(512)S(1)}, f32[512]{0:T(512)S(1)}, f32[512]{0:T(512)S(1)}) fusion(pred[1536]{0:T(1024)(128)(4,1)S(1)} %get-tuple-element.121, pred[1536]{0:T(1024)(128)(4,1)S(1)} %get-tuple-element.122, ...), kind=kOutput, calls=%fused_computation.2.clone.1 | convolution fusion | flops 213905408 | bytes 557060 | tf_op jit(solution)/shard_map/while/body/eval_jaxpr/re,se->rs/dot_general | solution.py:17
  83.6 0.1 stack.35
  84.3 0.1 multiply_reduce_fusion.3
  84.5 2.5 %select_reduce_fusion.9 = (f32[512]{0:T(512)S(1)}, f32[512]{0:T(512)S(1)}, f32[512]{0:T(512)S(1)}, f32[512]{0:T(512)S(1)}, f32[512]{0:T(512)S(1)}, /*index=5*/f32[512]{0:T(512)S(1)}, f32[512]{0:T(512)S(1)}, f32[512]{0:T(512)S(1)}) fusion(pred[1536]{0:T(1024)(128)(4,1)S(1)} %get-tuple-element.121, pred[1536]{0:T(1024)(128)(4,1)S(1)} %get-tuple-element.122, ...), kind=kOutput, calls=%fused_computation.2.clone.1 | convolution fusion | flops 213905408 | bytes 557060 | tf_op jit(solution)/shard_map/while/body/eval_jaxpr/re,se->rs/dot_general | solution.py:17
  87.7 0.1 multiply_reduce_fusion.3
  87.9 0.7 reshape.111
  (96 shorter events, 3.0 us)
Async XLA Ops:
  0.0 15.4 %copy-start = (bf16[768,1536]{1,0:T(8,128)(2,1)S(1)}, bf16[768,1536]{1,0:T(8,128)(2,1)}, u32[]{:S(2)}) copy-start(bf16[768,1536]{1,0:T(8,128)(2,1)} %param.9) | copy-start | bytes 7077892
  8.1 14.5 %all-to-all-start = ((s32[8,192,1]{1,2,0:T(1,128)}), s32[8,192,1]{1,2,0:T(1,128)S(1)}, u32[]{:S(2)}, u32[]{:S(2)}) async-start(s32[8,192,1]{1,2,0:T(1,128)} %all_to_all.22), calls=%async_computation | async-start | bytes 16384 | tf_op jit(solution)/shard_map/all_to_all | solution.py:66
  15.4 13.2 %copy-start.3 = (u32[32]{0:T(128)S(1)}, u32[32]{0:T(128)}, u32[]{:S(2)}) copy-start(u32[32]{0:T(128)} %constant.55) | copy-start | bytes 388
  15.4 14.5 %copy-start.2 = (s32[8]{0:T(128)S(1)}, s32[8]{0:T(128)}, u32[]{:S(2)}) copy-start(s32[8]{0:T(128)} %param.15) | copy-start | bytes 100
  15.4 27.3 %copy-start.1 = (bf16[8,32,128]{2,1,0:T(8,128)(2,1)S(1)}, bf16[8,32,128]{2,1,0:T(8,128)(2,1)}, u32[]{:S(2)}) copy-start(bf16[8,32,128]{2,1,0:T(8,128)(2,1)} %param.14) | copy-start | bytes 196612
  22.6 51.7 %all-to-all-start.1 = ((bf16[8,192,128]{2,1,0:T(8,128)(2,1)}), bf16[8,192,128]{2,1,0:T(8,128)(2,1)S(1)}, u32[]{:S(2)}, u32[]{:S(2)}) async-start(bf16[8,192,128]{2,1,0:T(8,128)(2,1)} %bitcast.7), calls=%async_computation.1 | async-start | bytes 786432 | tf_op jit(solution)/shard_map/all_to_all | solution.py:65
where the time goes:
time: 88.9 us; the launch traced here: 88.6 us
  blocking collectives  44 us (49%)
  local copies, waits for them, and re-layouts  14.1 us (16%)
  starting transfers between devices  13.3 us (15%)
  matrix products  11.9 us (13%)
  other arithmetic  4.34 us (5%)
    all_gather x1, blocking collectives, shards(): lax.all_gather(query_tokens, 'blk', axis=0, tiled=True)  31.5 us
    unnamed x1, blocking collectives  12.5 us
    dot_general x4, matrix products, page_maxsim(): jnp.einsum('re,se->rs', tokens, embedded, preferred_element_type=jnp.floa...  9.97 us
    all_to_all x1, starting transfers between devices, shards(): lax.all_to_all(outgoing_pages, 'blk', split_axis=0, concat_axis=0, tiled=...  7.31 us
    all_to_all x1, starting transfers between devices, shards(): lax.all_to_all(packed, 'blk', split_axis=0, concat_axis=0, tiled=True)  5.99 us
    scatter x1, local copies, waits for them, and re-layouts, shards(): jnp.zeros((slot_count, local.shape[1]), jnp.bfloat16).at[slot_index]  4.98 us
    scatter x1, local copies, waits for them, and re-layouts, shards(): jnp.full((slot_count,), -1, jnp.int32).at[slot_index].set(page_ids)  3.54 us
    another operation x36, local copies, waits for them, and re-layouts, page_maxsim(): jnp.stack([jnp.max(jnp.where(slot_pages[None, :] == page, sims, jnp.float...  2.46 us
  transfers between devices with their start and end apart: 2, of which 0 were waited for; matrix products, arithmetic and copies ran while one was open for 9% of the time, Pallas kernels for 0%

commit v1 on v0

--- a/solution.py
+++ b/solution.py
@@ -5,6 +5,37 @@
 from jax.sharding import PartitionSpec as P
 
 PAGES_DEV = 8
+
+
+def edge_hold(vec, row_dim, sample):
+    s_next, carry_in = (vec.shape[:row_dim], vec.shape[row_dim + 1 :])
+    oldest = vec.reshape(*s_next, sample, -1, *carry_in)
+    return jnp.moveaxis(oldest, row_dim, 0)
+
+
+def carry_notes_in(buf, pos_dim):
+    buf = jnp.moveaxis(buf, 0, pos_dim)
+    mid_arr = buf.shape
+    return buf.reshape(
+        *mid_arr[:pos_dim], mid_arr[pos_dim] * mid_arr[pos_dim + 1], *mid_arr[pos_dim + 2 :]
+    )
+
+
+def put_pairs_all(block_in, axis_tag, vals, matrix=0):
+    base_arr = lax.axis_size(axis_tag)
+    after = lax.axis_index(axis_tag)
+    v_next, state_next = (base_arr, after)
+    back = edge_hold(block_in, vals, v_next)
+    buffer = [back[state_next]]
+    for to_i in tuple(range(1, v_next)):
+        t1 = back[state_next ^ to_i]
+        e_now = lax.ppermute(
+            t1, axis_name=axis_tag, perm=[(nth, nth ^ to_i) for nth in range(v_next)]
+        )
+        buffer.append(e_now)
+    upper = jnp.stack(buffer)
+    back = upper[state_next ^ jnp.arange(v_next)]
+    return carry_notes_in(back, matrix)
 
 
 def embed(rows, weight, bias):
@@ -62,7 +93,7 @@
     local = embed(patch_rows, proj_weight, proj_bias)
     packed = jnp.zeros((slot_count, local.shape[1]), jnp.bfloat16).at[slot_index].set(local)
     embedded, slot_pages = (
-        lax.all_to_all(packed, "blk", split_axis=0, concat_axis=0, tiled=True),
+        put_pairs_all(packed, "blk", 0),
         lax.all_to_all(outgoing_pages, "blk", split_axis=0, concat_axis=0, tiled=True),
     )
     per_block = query_tokens.shape[0]

time: 88.9 us -> 107 us (1.20)
  local copies, waits for them, and re-layouts: 14.1 us -> 22.6 us
  starting transfers between devices: 13.3 us -> 19.1 us
  matrix products: 11.9 us -> 16.2 us
  blocking collectives: 44 us -> 42.8 us
    ppermute x0 -> x7, starting transfers between devices: none -> 14.2 us  [put_pairs_all(): lax.ppermute(t1, axis_name=axis_tag, perm=[(nth, nth ^ to_i) for nth in r...]
    all_to_all x1 -> x0, starting transfers between devices: 5.99 us -> none  [shards(): lax.all_to_all(packed, 'blk', split_axis=0, concat_axis=0, tiled=True)]
    dot_general x4, matrix products: 9.97 us -> 14.3 us  [page_maxsim(): jnp.einsum('re,se->rs', tokens, embedded, preferred_element_type=jnp.floa...]
    unnamed x11 -> x17, local copies, waits for them, and re-layouts: 0.92 us -> 4.99 us
    all_to_all x1, starting transfers between devices: 7.31 us -> 4.88 us  [shards(): lax.all_to_all(outgoing_pages, 'blk', split_axis=0, concat_axis=0, tiled=...]
    dynamic_update_slice x4, local copies, waits for them, and re-layouts: 0.03 us -> 2.39 us  [score_block(): scored = lax.map(one_block, (token_blocks, count_blocks))]
    unnamed x1, blocking collectives: 12.5 us -> 10.7 us
    gather x0 -> x1, local copies, waits for them, and re-layouts: none -> 1.33 us  [put_pairs_all(): back = upper[state_next ^ jnp.arange(v_next)]]
  transfers between devices with their start and end apart: 2 -> 8, of which waited for: 0 -> 0; matrix products, arithmetic and copies ran while one was open for 9% -> 8% of each run, Pallas kernels for 0% -> 0%
where the time goes in v1:
time: 107 us; the launch traced here: 106 us
  blocking collectives  42.8 us (40%)
  local copies, waits for them, and re-layouts  22.6 us (21%)
  starting transfers between devices  19.1 us (18%)
  matrix products  16.2 us (15%)
  other arithmetic  4.34 us (4%)
    all_gather x1, blocking collectives, shards(): lax.all_gather(query_tokens, 'blk', axis=0, tiled=True)  32 us
    dot_general x4, matrix products, page_maxsim(): jnp.einsum('re,se->rs', tokens, embedded, preferred_element_type=jnp.floa...  14.3 us
    ppermute x7, starting transfers between devices, put_pairs_all(): lax.ppermute(t1, axis_name=axis_tag, perm=[(nth, nth ^ to_i) for nth in r...  14.2 us
    unnamed x1, blocking collectives  10.7 us
    unnamed x17, local copies, waits for them, and re-layouts  4.99 us
    all_to_all x1, starting transfers between devices, shards(): lax.all_to_all(outgoing_pages, 'blk', split_axis=0, concat_axis=0, tiled=...  4.88 us
    scatter x1, local copies, waits for them, and re-layouts, shards(): jnp.zeros((slot_count, local.shape[1]), jnp.bfloat16).at[slot_index]  4.36 us
    scatter x1, local copies, waits for them, and re-layouts, shards(): jnp.full((slot_count,), -1, jnp.int32).at[slot_index].set(page_ids)  3.54 us
  transfers between devices with their start and end apart: 8, of which 0 were waited for; matrix products, arithmetic and copies ran while one was open for 8% of the time, Pallas kernels for 0%

profile of v1, /device:TPU:0, one launch (start us, length us, event | category | flops | bytes accessed | tf_op | source)
XLA Modules:
  0.0 106.1 jit_solution(1863148095681323449)
XLA Ops:
  0.0 0.8 reduce
  0.9 1.7 %reduce-window.6 = s32[8,6,128]{2,0,1:T(8,128)S(1)} reduce-window(s32[8,6,128]{2,0,1:T(8,128)S(1)} %fusion.10, s32[]{:T(128)} %copy.48), window={size=1x1x128 pad=0_0x0_0x127_0}, to_apply=%region_0.0 | reduce-window | flops 780288 | bytes 49156 | tf_op jit(solution)/shard_map/reduce-window
  3.1 0.7 fusion.13
  3.9 1.9 %multiply_reduce_fusion.1 = (f32[768]{0:T(1024)S(1)}, f32[768,128]{0,1:T(8,128)S(1)}) fusion(f32[128]{0:T(128)} %param.13, bf16[768,1536]{1,0:T(8,128)(2,1)S(1)} %copy-done, bf16[1536,128]{1,0:T(8,128)(2,1)} %param.12), kind=kOutput, calls=%fused_computation.39 | convolution fusion | flops 302284032 | bytes 3149312 | tf_op jit(solution)/shard_map/dot_general | solution.py:42
  6.1 4.4 %scatter_custom_fusion.1 = bf16[1536,128]{1,0:T(8,128)(2,1)S(1)} fusion(s32[768]{0:T(1024)S(1)} %fusion.13, bf16[768,128]{1,0:T(8,128)(2,1)S(1)} %copy.23, bf16[]{:T(256)} %constant.13.clone.1), kind=kCustom, calls=%fused_computation.40 | custom fusion | bytes 393218 | tf_op jit(solution)/shard_map/scatter | solution.py:94
  10.5 0.7 dynamic-slice_bitcast_fusion
  11.1 3.0 %collective-permute-start = (bf16[192,128]{1,0:T(8,128)(2,1)}, bf16[192,128]{1,0:T(8,128)(2,1)}, u32[]{:S(2)}, u32[]{:S(2)}) collective-permute-start(bf16[192,128]{1,0:T(8,128)(2,1)} %get-tuple-element.72), channel_id=1, source_target_pairs={{0,2},{2,0},{4,6},{6,4},{8,10},{10,8},{12,14},{14,12},{1,3},{3,1},... | collective-permute-start | bytes 147464 | tf_op jit(solution)/shard_map/ppermute | solution.py:32
  14.1 1.6 %collective-permute-start.1 = (bf16[192,128]{1,0:T(8,128)(2,1)}, bf16[192,128]{1,0:T(8,128)(2,1)}, u32[]{:S(2)}, u32[]{:S(2)}) collective-permute-start(bf16[192,128]{1,0:T(8,128)(2,1)} %get-tuple-element.71), channel_id=1, source_target_pairs={{0,4},{2,6},{4,0},{6,2},{8,12},{10,14},{12,8},{14,10},{1,5},{3,7},... | collective-permute-start | bytes 147464 | tf_op jit(solution)/shard_map/ppermute | solution.py:32
  15.7 3.0 %collective-permute-start.3 = (bf16[192,128]{1,0:T(8,128)(2,1)S(1)}, bf16[192,128]{1,0:T(8,128)(2,1)}, u32[]{:S(2)}, u32[]{:S(2)}) collective-permute-start(bf16[192,128]{1,0:T(8,128)(2,1)S(1)} %get-tuple-element.69), channel_id=1, source_target_pairs={{0,8},{2,10},{4,12},{6,14},{8,0},{10,2},{12,4},{14,6},{1,9},{3,11}... | collective-permute-start | bytes 147464 | tf_op jit(solution)/shard_map/ppermute | solution.py:32
  18.7 1.3 %collective-permute-start.4 = (bf16[192,128]{1,0:T(8,128)(2,1)S(1)}, bf16[192,128]{1,0:T(8,128)(2,1)}, u32[]{:S(2)}, u32[]{:S(2)}) collective-permute-start(bf16[192,128]{1,0:T(8,128)(2,1)S(1)} %get-tuple-element.68), channel_id=1, source_target_pairs={{0,10},{2,8},{4,14},{6,12},{8,2},{10,0},{12,6},{14,4},{1,11},{3,9}... | collective-permute-start | bytes 147464 | tf_op jit(solution)/shard_map/ppermute | solution.py:32
  20.0 3.5 %scatter_custom_fusion = s32[1536]{0:T(1024)S(1)} fusion(s32[768]{0:T(1024)S(1)} %fusion.13, s32[768]{0:T(1024)} %param.11, s32[]{:T(128)} %constant.27.clone.1), kind=kCustom, calls=%fused_computation.66 | custom fusion | bytes 6656 | tf_op jit(solution)/shard_map/scatter | solution.py:92
  23.5 0.7 all_to_all.11
  24.2 4.9 %all-to-all-start = ((s32[8,192,1]{1,2,0:T(1,128)}), s32[8,192,1]{1,2,0:T(1,128)S(1)}, u32[]{:S(2)}, u32[]{:S(2)}) async-start(s32[8,192,1]{1,2,0:T(1,128)} %all_to_all.11), calls=%async_computation | async-start | bytes 16384 | tf_op jit(solution)/shard_map/all_to_all | solution.py:97
  29.1 32.0 %all_gather.6 = bf16[64,32,128]{2,1,0:T(8,128)(2,1)S(1)} all-gather(bf16[8,32,128]{2,1,0:T(8,128)(2,1)S(1)} %copy-done.1), channel_id=1, replica_groups=mesh['groups'=2,'blk'=8,'inner'=2] {'blk'}, dimensions={0}, use_global_device_ids=true | all-gather | bytes 589824 | tf_op jit(solution)/shard_map/all_gather | solution.py:108
  61.2 0.7 dynamic-slice
  62.8 10.7 %all-reduce = s32[64]{0:T(128)S(1)} all-reduce(s32[64]{0:T(128)S(1)} %dynamic-update-slice), channel_id=1, replica_groups=mesh['groups'=2,'blk'=8,'inner'=2] {'blk'}, use_global_device_ids=true, to_apply=%add | all-reduce | flops 64 | bytes 512
  73.7 1.1 %collective-permute-start.5 = (bf16[192,128]{1,0:T(8,128)(2,1)S(1)}, bf16[192,128]{1,0:T(8,128)(2,1)S(1)}, u32[]{:S(2)}, u32[]{:S(2)}) collective-permute-start(bf16[192,128]{1,0:T(8,128)(2,1)S(1)} %get-tuple-element.67), channel_id=1, source_target_pairs={{0,12},{2,14},{4,8},{6,10},{8,4},{10,6},{12,0},{14,2},{1,13},{3,15... | collective-permute-start | bytes 147464 | tf_op jit(solution)/shard_map/ppermute | solution.py:32
  74.8 0.8 bitcast_dynamic-update-slice_fusion.7
  75.7 4.2 %collective-permute-start.6 = (bf16[192,128]{1,0:T(8,128)(2,1)S(1)}, bf16[192,128]{1,0:T(8,128)(2,1)S(1)}, u32[]{:S(2)}, u32[]{:S(2)}) collective-permute-start(bf16[192,128]{1,0:T(8,128)(2,1)S(1)} %get-tuple-element.66), channel_id=1, source_target_pairs={{0,14},{2,12},{4,10},{6,8},{8,6},{10,4},{12,2},{14,0},{1,15},{3,13... | collective-permute-start | bytes 147464 | tf_op jit(solution)/shard_map/ppermute | solution.py:32
  79.9 0.8 bitcast_dynamic-update-slice_fusion.6
  80.7 0.8 bitcast_dynamic-update-slice_fusion.5
  81.5 0.8 bitcast_dynamic-update-slice_fusion.4
  82.3 0.8 bitcast_dynamic-update-slice_fusion.3
  83.2 1.3 %gather_fusion = bf16[8,192,128]{2,1,0:T(8,128)(2,1)} fusion(bf16[8,192,128]{2,1,0:T(8,128)(2,1)S(1)} %bitcast_dynamic-update-slice_fusion.1, s32[1024]{0:T(1024)S(1)} %pad_clamp_fusion), kind=kCustom, calls=%fused_computation | custom fusion | bytes 786464 | tf_op jit(solution)/shard_map/gather | solution.py:37
  84.5 20.2 %while.10 = (s32[]{:T(128)}, f32[4,8,16]{2,1,0:T(8,128)}, s32[1536]{0:T(1024)S(1)}, bf16[4,512,128]{2,1,0:T(8,128)(2,1)S(1)}, bf16[1536,128]{1,0:T(8,128)(2,1)}, /*index=5*/s32[4,16]{1,0:T(4,128)S(1)}, s32[]{:T(128)}) while((s32[]{:T(128)}, f32[4,8,16]{2,1,0:T(8,128)}, s32[1536]{0:T(1024)S(1)}, bf16[4,512,128]{2,1,0:T(8,128)(2,1)S(1)}, ...), condition=%wide.region_16.17_spmd, body=%wide.region_6.16_spmd.sunk | while | flops 213926784 | bytes 759573 | solution.py:76
  84.5 3.6 %select_reduce_fusion.9 = (f32[512]{0:T(512)S(1)}, f32[512]{0:T(512)S(1)}, f32[512]{0:T(512)S(1)}, f32[512]{0:T(512)S(1)}, f32[512]{0:T(512)S(1)}, /*index=5*/f32[512]{0:T(512)S(1)}, f32[512]{0:T(512)S(1)}, f32[512]{0:T(512)S(1)}) fusion(pred[1536]{0:T(1024)(128)(4,1)S(1)} %get-tuple-element.129, pred[1536]{0:T(1024)(128)(4,1)S(1)} %get-tuple-element.130, ...), kind=kOutput, calls=%fused_computation.3.clone.1 | convolution fusion | flops 213905408 | bytes 557060 | tf_op jit(solution)/shard_map/while/body/eval_jaxpr/re,se->rs/dot_general | solution.py:48
  89.6 3.6 %select_reduce_fusion.9 = (f32[512]{0:T(512)S(1)}, f32[512]{0:T(512)S(1)}, f32[512]{0:T(512)S(1)}, f32[512]{0:T(512)S(1)}, f32[512]{0:T(512)S(1)}, /*index=5*/f32[512]{0:T(512)S(1)}, f32[512]{0:T(512)S(1)}, f32[512]{0:T(512)S(1)}) fusion(pred[1536]{0:T(1024)(128)(4,1)S(1)} %get-tuple-element.129, pred[1536]{0:T(1024)(128)(4,1)S(1)} %get-tuple-element.130, ...), kind=kOutput, calls=%fused_computation.3.clone.1 | convolution fusion | flops 213905408 | bytes 557060 | tf_op jit(solution)/shard_map/while/body/eval_jaxpr/re,se->rs/dot_general | solution.py:48
  94.6 3.6 %select_reduce_fusion.9 = (f32[512]{0:T(512)S(1)}, f32[512]{0:T(512)S(1)}, f32[512]{0:T(512)S(1)}, f32[512]{0:T(512)S(1)}, f32[512]{0:T(512)S(1)}, /*index=5*/f32[512]{0:T(512)S(1)}, f32[512]{0:T(512)S(1)}, f32[512]{0:T(512)S(1)}) fusion(pred[1536]{0:T(1024)(128)(4,1)S(1)} %get-tuple-element.129, pred[1536]{0:T(1024)(128)(4,1)S(1)} %get-tuple-element.130, ...), kind=kOutput, calls=%fused_computation.3.clone.1 | convolution fusion | flops 213905408 | bytes 557060 | tf_op jit(solution)/shard_map/while/body/eval_jaxpr/re,se->rs/dot_general | solution.py:48
  99.6 3.6 %select_reduce_fusion.9 = (f32[512]{0:T(512)S(1)}, f32[512]{0:T(512)S(1)}, f32[512]{0:T(512)S(1)}, f32[512]{0:T(512)S(1)}, f32[512]{0:T(512)S(1)}, /*index=5*/f32[512]{0:T(512)S(1)}, f32[512]{0:T(512)S(1)}, f32[512]{0:T(512)S(1)}) fusion(pred[1536]{0:T(1024)(128)(4,1)S(1)} %get-tuple-element.129, pred[1536]{0:T(1024)(128)(4,1)S(1)} %get-tuple-element.130, ...), kind=kOutput, calls=%fused_computation.3.clone.1 | convolution fusion | flops 213905408 | bytes 557060 | tf_op jit(solution)/shard_map/while/body/eval_jaxpr/re,se->rs/dot_general | solution.py:48
  104.1 0.6 bitcast_dynamic-update-slice_fusion.9
  104.7 0.7 copy.24
  105.4 0.7 reshape.133
  (119 shorter events, 6.4 us)
Async XLA Ops:
  0.0 3.8 %copy-start = (bf16[768,1536]{1,0:T(8,128)(2,1)S(1)}, bf16[768,1536]{1,0:T(8,128)(2,1)}, u32[]{:S(2)}) copy-start(bf16[768,1536]{1,0:T(8,128)(2,1)} %param.9) | copy-start | bytes 7077892
  3.8 25.3 %copy-start.1 = (bf16[8,32,128]{2,1,0:T(8,128)(2,1)S(1)}, bf16[8,32,128]{2,1,0:T(8,128)(2,1)}, u32[]{:S(2)}) copy-start(bf16[8,32,128]{2,1,0:T(8,128)(2,1)} %param.14) | copy-start | bytes 196612
  3.9 57.3 %copy-start.3 = (u32[32]{0:T(128)S(1)}, u32[32]{0:T(128)}, u32[]{:S(2)}) copy-start(u32[32]{0:T(128)} %constant.79) | copy-start | bytes 388
  3.9 58.7 %copy-start.2 = (s32[8]{0:T(128)S(1)}, s32[8]{0:T(128)}, u32[]{:S(2)}) copy-start(s32[8]{0:T(128)} %param.15) | copy-start | bytes 100
  11.1 62.6 %collective-permute-start = (bf16[192,128]{1,0:T(8,128)(2,1)}, bf16[192,128]{1,0:T(8,128)(2,1)}, u32[]{:S(2)}, u32[]{:S(2)}) collective-permute-start(bf16[192,128]{1,0:T(8,128)(2,1)} %get-tuple-element.72), channel_id=1, source_target_pairs={{0,2},{2,0},{4,6},{6,4},{8,10},{10,8},{12,14},{14,12},{1,3},{3,1},... | collective-permute-start | bytes 147464 | tf_op jit(solution)/shard_map/ppermute | solution.py:32
  14.1 61.5 %collective-permute-start.1 = (bf16[192,128]{1,0:T(8,128)(2,1)}, bf16[192,128]{1,0:T(8,128)(2,1)}, u32[]{:S(2)}, u32[]{:S(2)}) collective-permute-start(bf16[192,128]{1,0:T(8,128)(2,1)} %get-tuple-element.71), channel_id=1, source_target_pairs={{0,4},{2,6},{4,0},{6,2},{8,12},{10,14},{12,8},{14,10},{1,5},{3,7},... | collective-permute-start | bytes 147464 | tf_op jit(solution)/shard_map/ppermute | solution.py:32
  15.7 65.0 %collective-permute-start.2 = (bf16[192,128]{1,0:T(8,128)(2,1)}, bf16[192,128]{1,0:T(8,128)(2,1)}, u32[]{:S(2)}, u32[]{:S(2)}) collective-permute-start(bf16[192,128]{1,0:T(8,128)(2,1)} %get-tuple-element.70), channel_id=1, source_target_pairs={{0,6},{2,4},{4,2},{6,0},{8,14},{10,12},{12,10},{14,8},{1,7},{3,5},... | collective-permute-start | bytes 147464 | tf_op jit(solution)/shard_map/ppermute | solution.py:32
  15.7 65.8 %collective-permute-start.3 = (bf16[192,128]{1,0:T(8,128)(2,1)S(1)}, bf16[192,128]{1,0:T(8,128)(2,1)}, u32[]{:S(2)}, u32[]{:S(2)}) collective-permute-start(bf16[192,128]{1,0:T(8,128)(2,1)S(1)} %get-tuple-element.69), channel_id=1, source_target_pairs={{0,8},{2,10},{4,12},{6,14},{8,0},{10,2},{12,4},{14,6},{1,9},{3,11}... | collective-permute-start | bytes 147464 | tf_op jit(solution)/shard_map/ppermute | solution.py:32
  18.7 63.6 %collective-permute-start.4 = (bf16[192,128]{1,0:T(8,128)(2,1)S(1)}, bf16[192,128]{1,0:T(8,128)(2,1)}, u32[]{:S(2)}, u32[]{:S(2)}) collective-permute-start(bf16[192,128]{1,0:T(8,128)(2,1)S(1)} %get-tuple-element.68), channel_id=1, source_target_pairs={{0,10},{2,8},{4,14},{6,12},{8,2},{10,0},{12,6},{14,4},{1,11},{3,9}... | collective-permute-start | bytes 147464 | tf_op jit(solution)/shard_map/ppermute | solution.py:32
  24.2 49.4 %all-to-all-start = ((s32[8,192,1]{1,2,0:T(1,128)}), s32[8,192,1]{1,2,0:T(1,128)S(1)}, u32[]{:S(2)}, u32[]{:S(2)}) async-start(s32[8,192,1]{1,2,0:T(1,128)} %all_to_all.11), calls=%async_computation | async-start | bytes 16384 | tf_op jit(solution)/shard_map/all_to_all | solution.py:97
  73.7 9.4 %collective-permute-start.5 = (bf16[192,128]{1,0:T(8,128)(2,1)S(1)}, bf16[192,128]{1,0:T(8,128)(2,1)S(1)}, u32[]{:S(2)}, u32[]{:S(2)}) collective-permute-start(bf16[192,128]{1,0:T(8,128)(2,1)S(1)} %get-tuple-element.67), channel_id=1, source_target_pairs={{0,12},{2,14},{4,8},{6,10},{8,4},{10,6},{12,0},{14,2},{1,13},{3,15... | collective-permute-start | bytes 147464 | tf_op jit(solution)/shard_map/ppermute | solution.py:32
  75.7 7.5 %collective-permute-start.6 = (bf16[192,128]{1,0:T(8,128)(2,1)S(1)}, bf16[192,128]{1,0:T(8,128)(2,1)S(1)}, u32[]{:S(2)}, u32[]{:S(2)}) collective-permute-start(bf16[192,128]{1,0:T(8,128)(2,1)S(1)} %get-tuple-element.66), channel_id=1, source_target_pairs={{0,14},{2,12},{4,10},{6,8},{8,6},{10,4},{12,2},{14,0},{1,15},{3,13... | collective-permute-start | bytes 147464 | tf_op jit(solution)/shard_map/ppermute | solution.py:32
